TPU v7x, 256 devices: a whole 4x4x8 slice. The times are simulated.
256 devices in a mesh: dp: 16 (over y_hi, z), seq: 16 (over x, y_lo, core).
Axes of the slice: x: 4, y: 4 (y_hi: 2, y_lo: 2; y = y_hi * 2 + y_lo), z: 8, core: 2. Of those that a mesh axis runs over, the one named last changes fastest.
Arguments:
- queries: bfloat16 [16, 2048, 2048], P('dp', 'seq'), may hold values from -6 to 6
- key_states: bfloat16 [16, 2048, 2048], P('dp', 'seq'), may hold values from -6 to 6
- value_states: bfloat16 [16, 2048, 2048], P('dp', 'seq'), may hold values from -6 to 6
- cotangent: bfloat16 [16, 2048, 2048], P('dp', 'seq'), may hold values from -6 to 6
- filter_taps: float32 [7, 2048], replicated, may hold values from -3 to 3
Outputs:
- conv_output: bfloat16 [16, 2048, 2048], P('dp', 'seq')
- grad_queries: bfloat16 [16, 2048, 2048], P('dp', 'seq')
- grad_keys: bfloat16 [16, 2048, 2048], P('dp', 'seq')
- grad_values: bfloat16 [16, 2048, 2048], P('dp', 'seq')
- filter_gradient: float32 [7, 2048], replicated
All inputs are finite; a program needn't handle non-finite values.
Results may differ from a plain program's by a relative error of at most 0.015.
Values may be sent and summed in bfloat16 or wider, within the bound.
No kernel may reach another device: no remote copies, remote signals or barrier semaphores. Data moves between devices by JAX's collectives and lax.ppermute only.
A program may use at most 128 MiB of HBM per device.

v0:
```python
import jax
import jax.numpy as jnp
from jax import lax
from jax.sharding import PartitionSpec as P

HD = 128
TAPS = 7


def padded(value, width):
    peers = lax.axis_size("seq")
    length = value.shape[0]
    up = [(i, (i + 1) % peers) for i in range(peers)]
    down = [(j, i) for i, j in up]
    before = lax.ppermute(value[length - width :], "seq", up)
    after = lax.ppermute(value[:width], "seq", down)
    return jnp.concatenate([before, value, after], axis=0)


def butterfly_sum(value):
    axes = ("dp", "seq")
    peers = lax.axis_size("dp") * lax.axis_size("seq")
    bit = 1
    while bit < peers:
        pairs = [(i, i ^ bit) for i in range(peers)]
        value = value + lax.ppermute(value, axes, pairs)
        bit *= 2
    return value


def butterfly_gather(value):
    peers = lax.axis_size("seq")
    index = lax.axis_index("seq")
    bit = 1
    while bit < peers:
        pairs = [(i, i ^ bit) for i in range(peers)]
        other = lax.ppermute(value, "seq", pairs)
        upper = (index & bit) != 0
        value = jnp.where(
            upper,
            jnp.concatenate([other, value], axis=0),
            jnp.concatenate([value, other], axis=0),
        )
        bit *= 2
    return value


def on_device(queries, key_states, value_states, cotangent, filter_taps):
    tok_rows = queries.shape[1]
    channels = queries.shape[2]
    peers = lax.axis_size("seq")
    seq_total = tok_rows * peers
    head_count = channels // HD
    score_scale = HD ** (-0.5)
    half_width = (TAPS - 1) // 2
    local_q = queries[0]
    local_k = key_states[0]
    local_v = value_states[0]
    local_g = cotangent[0]
    grad_pad = padded(local_g, half_width)
    grad_sum = jnp.zeros((tok_rows, channels), jnp.float32)
    for tap_index in range(TAPS):
        start_row = 2 * half_width - tap_index
        grad_sum = grad_sum + filter_taps[tap_index] * grad_pad[
            start_row : start_row + tok_rows
        ].astype(jnp.float32)
    grad_attn = grad_sum.astype(jnp.bfloat16)

    def head_major(matrix):
        return matrix.reshape(tok_rows, head_count, HD).transpose(1, 0, 2)

    k_heads = lax.all_gather(head_major(local_k), "seq", axis=1, tiled=True)
    k_heads, local_v = lax.optimization_barrier((k_heads, local_v))
    v_heads = lax.all_gather(head_major(local_v), "seq", axis=1, tiled=True)

    q_heads = local_q.reshape(tok_rows, head_count, HD)
    d_heads = grad_attn.reshape(tok_rows, head_count, HD)

    device_index = lax.axis_index("seq")
    own_pos = device_index * tok_rows + jnp.arange(tok_rows, dtype=jnp.int32)
    all_pos = jnp.arange(seq_total, dtype=jnp.int32)
    visible = own_pos[:, None] >= all_pos[None, :]

    scores = (
        jnp.einsum("thd,hud->htu", q_heads, k_heads, preferred_element_type=jnp.float32)
        * score_scale
    )
    row_top = jnp.max(jnp.where(visible, scores, -jnp.inf), -1, keepdims=True)
    row_top, local_q2 = lax.optimization_barrier((row_top, local_q))
    qa_heads = lax.all_gather(head_major(local_q2), "seq", axis=1, tiled=True)
    raw = jnp.where(visible, jnp.exp(scores - row_top), 0.0)
    row_total = jnp.sum(raw, -1, keepdims=True)
    probs = raw / row_total
    probs_low = probs.astype(jnp.bfloat16)
    probs_low, grad_attn2 = lax.optimization_barrier((probs_low, grad_attn))
    da_heads = lax.all_gather(head_major(grad_attn2), "seq", axis=1, tiled=True)
    attended = jnp.einsum("htu,hud->thd", probs_low, v_heads, preferred_element_type=jnp.float32)
    attn_out = attended.astype(jnp.bfloat16).reshape(tok_rows, channels)
    dprob = jnp.einsum("thd,hud->htu", d_heads, v_heads, preferred_element_type=jnp.float32)
    row_delta = jnp.sum(probs * dprob, -1, keepdims=True)
    dscore = (probs * (dprob - row_delta) * score_scale).astype(jnp.bfloat16)
    grad_q = jnp.einsum("htu,hud->thd", dscore, k_heads, preferred_element_type=jnp.float32)
    grad_queries = grad_q.astype(jnp.bfloat16).reshape(tok_rows, channels)

    stats = jnp.stack([row_top[..., 0], row_total[..., 0], row_delta[..., 0]], 0)
    stats = butterfly_gather(stats.transpose(2, 0, 1)).transpose(1, 0, 2)
    top_all = stats[0].T[:, None, :]
    total_all = stats[1].T[:, None, :]
    delta_all = stats[2].T[:, None, :]

    kq_heads = head_major(local_k)
    kv_heads = head_major(local_v)
    key_visible = all_pos[None, :] >= own_pos[:, None]
    scores_t = (
        jnp.einsum("hud,htd->hut", kq_heads, qa_heads, preferred_element_type=jnp.float32)
        * score_scale
    )
    raw_t = jnp.where(key_visible, jnp.exp(scores_t - top_all), 0.0)
    probs_t = raw_t / total_all
    probs_low_t = probs_t.astype(jnp.bfloat16)
    dprob_t = jnp.einsum("hud,htd->hut", kv_heads, da_heads, preferred_element_type=jnp.float32)
    dscore_t = (probs_t * (dprob_t - delta_all) * score_scale).astype(jnp.bfloat16)
    grad_k = jnp.einsum("hut,htd->uhd", dscore_t, qa_heads, preferred_element_type=jnp.float32)
    grad_v = jnp.einsum("hut,htd->uhd", probs_low_t, da_heads, preferred_element_type=jnp.float32)
    grad_keys = grad_k.astype(jnp.bfloat16).reshape(tok_rows, channels)
    grad_values = grad_v.astype(jnp.bfloat16).reshape(tok_rows, channels)

    out_pad = padded(attn_out, half_width)
    conv_sum = jnp.zeros((tok_rows, channels), jnp.float32)
    filter_rows = []
    local_gf = local_g.astype(jnp.float32)
    for tap_index in range(TAPS):
        moved = out_pad[tap_index : tap_index + tok_rows].astype(jnp.float32)
        conv_sum = conv_sum + filter_taps[tap_index] * moved
        filter_rows.append(jnp.sum(moved * local_gf, 0))
    filter_gradient = butterfly_sum(jnp.stack(filter_rows, 0))
    conv_output = conv_sum.astype(jnp.bfloat16)
    return (
        conv_output[None],
        grad_queries[None],
        grad_keys[None],
        grad_values[None],
        filter_gradient,
    )


def solution(mesh):
    block = P("dp", "seq", None)
    in_specs = (block, block, block, block, P())
    out_specs = (block, block, block, block, P())
    return jax.shard_map(
        on_device, mesh=mesh, in_specs=in_specs, out_specs=out_specs, check_vma=False
    )
```

profile of v0, /device:TPU:1, one launch (start us, length us, event | category | flops | bytes accessed | tf_op | source)
XLA Modules:
  0.0 298.6 jit_solution(1885777955495145412)
XLA Ops:
  7.2 1.1 copy.119
  8.4 0.9 copy.127
  9.4 1.3 copy.80
  10.7 58.6 %all-gather.5.cloned.1.call-done = bf16[16,2048,128]{2,1,0:T(8,128)(2,1)} async-done(((bf16[16,128,128]{2,1,0:T(8,128)(2,1)}), bf16[16,2048,128]{2,1,0:T(8,128)(2,1)}) %all-gather.5.cloned.1.call-update) | async-done | bytes 8388624 | tf_op jit(solution)/shard_map/all_gather | solution.py:72
  69.3 1.0 copy.81
  70.4 1.3 copy.83
  71.7 1.1 copy.120
  72.9 1.0 iota_compare_fusion
  73.9 11.8 %fusion.1 = (f32[16,128]{1,0:T(8,128)S(1)}, f32[16,2048,128]{2,1,0:T(8,128)}) fusion(pred[128,2048]{0,1:T(8,128)(4,1)S(1)} %get-tuple-element.63, bf16[16,2048,128]{2,1,0:T(8,128)(2,1)} %all-gather.5.cloned.1.call-done, bf16[128,16,128]{2,1,0:T(8,128)(2,1)S(1)} %bitcast.140), kind=kOutput, calls=%fused_computation.4 | convolution fusion | flops 1086322688 | bytes 25960448 | tf_op jit(solution)/shard_map/thd,hud->htu/dot_general | solution.py:85
  85.7 1.0 copy.96
  87.3 1.4 collective-permute-start.1
  88.9 22.6 %collective-permute-done.1 = bf16[3,2048]{0,1:T(8,128)(2,1)S(1)} collective-permute-done((bf16[3,2048]{0,1:T(8,128)(2,1)S(1)}, bf16[3,2048]{0,1:T(8,128)(2,1)S(1)}, u32[]{:S(2)}, u32[]{:S(2)}) %collective-permute-start.1) | collective-permute-done | bytes 12320 | tf_op jit(solution)/shard_map/ppermute | solution.py:15
  111.5 3.1 %collective-permute-done = bf16[3,2048]{0,1:T(8,128)(2,1)S(1)} collective-permute-done((bf16[3,2048]{0,1:T(8,128)(2,1)S(1)}, bf16[3,2048]{0,1:T(8,128)(2,1)S(1)}, u32[]{:S(2)}, u32[]{:S(2)}) %collective-permute-start) | collective-permute-done | bytes 12320 | tf_op jit(solution)/shard_map/ppermute | solution.py:16
  114.7 3.7 %fusion.33 = bf16[128,2048]{0,1:T(8,128)(2,1)S(1)} fusion(bf16[128,2048]{0,1:T(8,128)(2,1)S(1)} %bitcast.122, bf16[3,2048]{0,1:T(8,128)(2,1)S(1)} %collective-permute-done.1, bf16[3,2048]{0,1:T(8,128)(2,1)S(1)} %collective-permute-done, f32[2048]{0:T(1024)S(1)} %bitcast.152, f32[2048]{0:T(1024)S(1)} %bitcast.154, f32[2048]{0:T(1024)S(1)} %bitcast.144, ...), kind=kLoop, calls=%fused_computation.66 | loop fusion | flops 10223616 | bytes 1130496 | tf_op jit(solution)/shard_map/convert_element_type | solution.py:67
  118.4 9.5 %fusion.5 = f32[16,128]{1,0:T(8,128)S(1)} fusion(f32[16,2048,128]{2,1,0:T(8,128)} %get-tuple-element.65, f32[16,128]{1,0:T(8,128)S(1)} %get-tuple-element.64, pred[128,2048]{0,1:T(8,128)(4,1)S(1)} %get-tuple-element.63), kind=kLoop, calls=%fused_computation.11 | loop fusion | flops 16775168 | bytes 17055744 | tf_op jit(solution)/shard_map/reduce_sum | solution.py:92
  127.9 10.6 %all-gather.7.cloned.1.call-done = bf16[16,2048,128]{2,1,0:T(8,128)(2,1)} async-done(((bf16[16,128,128]{2,1,0:T(8,128)(2,1)}), bf16[16,2048,128]{2,1,0:T(8,128)(2,1)}) %all-gather.7.cloned.1.call-update) | async-done | bytes 8388624 | tf_op jit(solution)/shard_map/all_gather | solution.py:74
  138.5 16.0 %multiply_reduce_fusion = (f32[16,128]{1,0:T(8,128)S(1)}, bf16[16,128,2048]{1,2,0:T(8,128)(2,1)}, f32[16,128,2048]{1,2,0:T(8,128)}) fusion(f32[16,128]{1,0:T(8,128)S(1)} %fusion.5, f32[16,128]{1,0:T(8,128)S(1)} %get-tuple-element.64, f32[16,2048,128]{2,1,0:T(8,128)} %get-tuple-element.65, pred[128,2048]{0,1:T(8,128)(4,1)S(1)} %get-tuple-element.63, ...), kind=kOutput, calls=%fused_computation.9 | convolution fusion | flops 1103099904 | bytes 51142656 | tf_op jit(solution)/shard_map/thd,hud->htu/dot_general | solution.py:99
  154.5 1.0 copy.97
  155.7 8.8 %multiply_reduce_fusion.1 = (f32[16,128]{1,0:T(8,128)S(1)}, bf16[128,16,128]{2,0,1:T(8,128)(2,1)S(1)}) fusion(f32[128,16,128]{2,0,1:T(8,128)S(1)} %copy.104, bf16[16,2048,128]{2,1,0:T(8,128)(2,1)} %all-gather.7.cloned.1.call-done, bf16[16,128,2048]{1,2,0:T(8,128)(2,1)} %get-tuple-element.14), kind=kOutput, calls=%fused_computation.73 | convolution fusion | flops 1074788352 | bytes 18358272 | tf_op jit(solution)/shard_map/htu,hud->thd/dot_general | solution.py:97
  164.6 1.1 copy.90
  165.7 0.7 collective-permute-start.3
  167.0 19.5 %collective-permute-done.3 = bf16[3,2048]{0,1:T(8,128)(2,1)S(1)} collective-permute-done((bf16[3,2048]{0,1:T(8,128)(2,1)}, bf16[3,2048]{0,1:T(8,128)(2,1)S(1)}, u32[]{:S(2)}, u32[]{:S(2)}) %collective-permute-start.3) | collective-permute-done | bytes 12320 | tf_op jit(solution)/shard_map/ppermute | solution.py:16
  186.5 3.4 %fusion.39 = (f32[2048]{0:T(1024)S(1)}, f32[2048]{0:T(1024)S(1)}, f32[2048]{0:T(1024)S(1)}, f32[2048]{0:T(1024)S(1)}, f32[2048]{0:T(1024)S(1)}, /*index=5*/f32[2048]{0:T(1024)S(1)}) fusion(bf16[3,2048]{0,1:T(8,128)(2,1)S(1)} %collective-permute-done.3, bf16[128,2048]{0,1:T(8,128)(2,1)S(1)} %bitcast.125, bf16[1,128,2048]{1,2,0:T(8,128)(2,1)S(1)} %copy.84, ...), kind=kLoop, calls=%fused_computation.72 | loop fusion | flops 9687040 | bytes 1122304 | tf_op jit(solution)/shard_map/reduce_sum | solution.py:135
  190.1 0.5 collective-permute-start.4
  190.6 0.7 collective-permute-done.8
  191.7 1.3 collective-permute-start.5
  193.0 3.8 %collective-permute-done.9 = f32[7,2048]{1,0:T(8,128)S(1)} collective-permute-done((f32[7,2048]{1,0:T(8,128)S(1)}, f32[7,2048]{1,0:T(8,128)S(1)}, u32[]{:S(2)}, u32[]{:S(2)}) %collective-permute-start.9) | collective-permute-done | bytes 57376 | tf_op jit(solution)/shard_map/ppermute | solution.py:26
  196.9 2.0 collective-permute-done.5
  199.0 1.4 collective-permute-done.10
  200.5 2.4 collective-permute-start.11
  202.8 17.1 %fusion.20 = bf16[16,128,128]{2,1,0:T(8,128)(2,1)S(1)} fusion(bf16[16,2048,128]{2,1,0:T(8,128)(2,1)} %all-gather.5.cloned.1.call-done, f32[16,128,2048]{1,2,0:T(8,128)} %get-tuple-element.66, f32[16,128]{1,0:T(8,128)S(1)} %get-tuple-element.46, f32[16,2048,128]{2,1,0:T(8,128)} %get-tuple-element.65, f32[16,128]{1,0:T(8,128)S(1)} %fusion.5, ...), kind=kOutput, calls=%fused_computation.37 | convolution fusion | flops 1107558400 | bytes 42754048 | tf_op jit(solution)/shard_map/htu,hud->thd/dot_general | solution.py:102
  219.9 1.0 copy.106
  220.9 1.4 collective-permute-start.12
  222.3 1.0 collective-permute-start.7
  223.3 1.2 collective-permute-done.12
  224.5 2.6 collective-permute-start.13
  227.1 3.7 %fusion.50 = bf16[1,128,2048]{1,2,0:T(8,128)(2,1)S(1)} fusion(f32[2048]{0:T(1024)S(1)} %bitcast.153, f32[2048]{0:T(1024)S(1)} %bitcast.155, f32[2048]{0:T(1024)S(1)} %bitcast.145, bf16[128,2048]{0,1:T(8,128)(2,1)S(1)} %bitcast.126, f32[2048]{0:T(1024)S(1)} %bitcast.147, f32[2048]{0:T(1024)S(1)} %bitcast.149, f32[2048]{0:T(1024)S(1)} %bitcast.151, ...), kind=kLoop, calls=%fused_computation.93 | loop fusion | flops 10223616 | bytes 1130496 | tf_op jit(solution)/shard_map/broadcast_in_dim | solution.py:139
  230.9 1.0 copy.105
  231.9 3.7 %collective-permute-start.14 = (f32[7,2048]{1,0:T(8,128)S(1)}, f32[7,2048]{1,0:T(8,128)S(1)}, u32[]{:S(2)}, u32[]{:S(2)}) collective-permute-start(f32[7,2048]{1,0:T(8,128)S(1)} %add.89), channel_id=1, source_target_pairs={{0,64},{1,65},{2,66},{3,67},{4,68},{5,69},{6,70},{7,71},{8,72},{9,... | collective-permute-start | bytes 172040 | tf_op jit(solution)/shard_map/ppermute | solution.py:26
  235.7 3.3 %collective-permute-done.14 = f32[7,2048]{1,0:T(8,128)S(1)} collective-permute-done((f32[7,2048]{1,0:T(8,128)S(1)}, f32[7,2048]{1,0:T(8,128)S(1)}, u32[]{:S(2)}, u32[]{:S(2)}) %collective-permute-start.14) | collective-permute-done | bytes 57376 | tf_op jit(solution)/shard_map/ppermute | solution.py:26
  239.0 2.6 collective-permute-start.15
  241.7 15.0 %fusion = f32[16,128,2048]{1,2,0:T(8,128)} fusion(f32[16,2048]{1,0:T(8,128)S(1)} %get-tuple-element.53, f32[16,2048]{1,0:T(8,128)S(1)} %get-tuple-element.54, pred[128,2048]{0,1:T(8,128)(4,1)} %get-tuple-element.62, bf16[16,2048,128]{2,1,0:T(8,128)(2,1)} %all-gather.9.cloned.1.call-done, bf16[128,16,128]{2,1,0:T(8,128)(2,1)S(1)} %bitcast.131), kind=kOutput, calls=%fused_computation.1 | convolution fusion | flops 1090519040 | bytes 26214400 | tf_op jit(solution)/shard_map/hud,htd->hut/dot_general | solution.py:115
  256.6 0.6 add.91
  257.3 7.9 %all-gather.11.cloned.1.call-done = bf16[16,2048,128]{2,1,0:T(8,128)(2,1)} async-done(((bf16[16,128,128]{2,1,0:T(8,128)(2,1)}), bf16[16,2048,128]{2,1,0:T(8,128)(2,1)}) %all-gather.11.cloned.1.call-update) | async-done | bytes 8388624 | tf_op jit(solution)/shard_map/all_gather | solution.py:96
  265.2 13.5 %fusion.19 = bf16[16,128,128]{2,1,0:T(8,128)(2,1)S(1)} fusion(bf16[16,2048,128]{2,1,0:T(8,128)(2,1)} %all-gather.9.cloned.1.call-done, f32[16,128,2048]{1,2,0:T(8,128)} %fusion, f32[16,2048]{1,0:T(8,128)S(1)} %get-tuple-element.52, bf16[16,2048,128]{2,1,0:T(8,128)(2,1)} %all-gather.11.cloned.1.call-done, bf16[128,16,128]{2,0,1:T(8,128)(2,1)S(1)} %copy-done), kind=kOutput, calls=%fused_computation.35 | convolution fusion | flops 2164523008 | bytes 34734080 | tf_op jit(solution)/shard_map/hut,htd->uhd/dot_general | solution.py:123
  278.7 1.0 copy.107
  279.7 10.9 %fusion.16 = bf16[16,128,128]{2,1,0:T(8,128)(2,1)S(1)} fusion(bf16[16,2048,128]{2,1,0:T(8,128)(2,1)} %all-gather.11.cloned.1.call-done, f32[16,128,2048]{1,2,0:T(8,128)} %fusion), kind=kOutput, calls=%fused_computation.34 | convolution fusion | flops 1078198272 | bytes 25690112 | tf_op jit(solution)/shard_map/hut,htd->uhd/dot_general | solution.py:124
  290.7 1.0 copy.108
  (50 shorter events, 2.7 us)
Async XLA Ops:
  7.2 62.1 %all-gather.5.cloned.1.call-start = ((), (), s32[]{:S(2)}) async-start(), calls=%async_computation | async-start | bytes 8912896 | tf_op jit(solution)/shard_map/all_gather | solution.py:72
  9.3 129.2 %all-gather.7.cloned.1.call-start = ((), (), s32[]{:S(2)}) async-start(), calls=%async_computation.1 | async-start | bytes 8912896 | tf_op jit(solution)/shard_map/all_gather | solution.py:74
  70.3 171.3 %all-gather.9.cloned.1.call-start = ((), (), s32[]{:S(2)}) async-start(), calls=%async_computation.2 | async-start | bytes 8912896 | tf_op jit(solution)/shard_map/all_gather | solution.py:90
  73.9 12.9 %copy-start.1 = (bf16[1,128,2048]{2,1,0:T(8,128)(2,1)S(1)}, bf16[1,128,2048]{2,1,0:T(8,128)(2,1)}, u32[]{:S(2)}) copy-start(bf16[1,128,2048]{2,1,0:T(8,128)(2,1)} %param.8) | copy-start | bytes 1572868
  73.9 15.0 %copy-start.2 = (f32[7,2048]{1,0:T(8,128)S(1)}, f32[7,2048]{1,0:T(8,128)}, u32[]{:S(2)}) copy-start(f32[7,2048]{1,0:T(8,128)} %param.9) | copy-start | bytes 172036
  86.7 178.4 %all-gather.11.cloned.1.call-start = ((), (), s32[]{:S(2)}) async-start(), calls=%async_computation.3 | async-start | bytes 8912896 | tf_op jit(solution)/shard_map/all_gather | solution.py:96
  87.3 24.3 %collective-permute-start.1 = (bf16[3,2048]{0,1:T(8,128)(2,1)S(1)}, bf16[3,2048]{0,1:T(8,128)(2,1)S(1)}, u32[]{:S(2)}, u32[]{:S(2)}) collective-permute-start(bf16[3,2048]{0,1:T(8,128)(2,1)S(1)} %get-tuple-element.51), channel_id=1, source_target_pairs={{0,1},{1,2},{2,3},{3,4},{4,5},{5,6},{6,7},{7,8},{8,9},{9,10},{10,1... | collective-permute-start | bytes 36872 | tf_op jit(solution)/shard_map/ppermute | solution.py:15
  88.7 26.0 %collective-permute-start = (bf16[3,2048]{0,1:T(8,128)(2,1)S(1)}, bf16[3,2048]{0,1:T(8,128)(2,1)S(1)}, u32[]{:S(2)}, u32[]{:S(2)}) collective-permute-start(bf16[3,2048]{0,1:T(8,128)(2,1)S(1)} %get-tuple-element.50), channel_id=1, source_target_pairs={{1,0},{2,1},{3,2},{4,3},{5,4},{6,5},{7,6},{8,7},{9,8},{10,9},{11,1... | collective-permute-start | bytes 36872 | tf_op jit(solution)/shard_map/ppermute | solution.py:16
  164.6 2.1 collective-permute-start.2
  165.7 20.8 %collective-permute-start.3 = (bf16[3,2048]{0,1:T(8,128)(2,1)}, bf16[3,2048]{0,1:T(8,128)(2,1)S(1)}, u32[]{:S(2)}, u32[]{:S(2)}) collective-permute-start(bf16[3,2048]{0,1:T(8,128)(2,1)} %copy.90), channel_id=1, source_target_pairs={{1,0},{2,1},{3,2},{4,3},{5,4},{6,5},{7,6},{8,7},{9,8},{10,9},{11,1... | collective-permute-start | bytes 36872 | tf_op jit(solution)/shard_map/ppermute | solution.py:16
  190.0 1.3 collective-permute-start.8
  190.1 1.5 collective-permute-start.4
  191.3 5.5 %collective-permute-start.9 = (f32[7,2048]{1,0:T(8,128)S(1)}, f32[7,2048]{1,0:T(8,128)S(1)}, u32[]{:S(2)}, u32[]{:S(2)}) collective-permute-start(f32[7,2048]{1,0:T(8,128)S(1)} %add.84), channel_id=1, source_target_pairs={{0,2},{1,3},{2,0},{3,1},{4,6},{5,7},{6,4},{7,5},{8,10},{9,11},{10,... | collective-permute-start | bytes 172040 | tf_op jit(solution)/shard_map/ppermute | solution.py:26
  191.7 7.3 %collective-permute-start.5 = (f32[256,3,16]{0,2,1:T(8,128)S(1)}, f32[256,3,16]{0,2,1:T(8,128)S(1)}, u32[]{:S(2)}, u32[]{:S(2)}) collective-permute-start(f32[256,3,16]{0,2,1:T(8,128)S(1)} %maximum_select_fusion.3), channel_id=1, source_target_pairs={{0,2},{1,3},{2,0},{3,1},{4,6},{5,7},{6,4},{7,5},{8,10},{9,11},{10,... | collective-permute-start | bytes 147464 | tf_op jit(solution)/shard_map/ppermute | solution.py:37
  196.8 3.6 %collective-permute-start.10 = (f32[7,2048]{1,0:T(8,128)S(1)}, f32[7,2048]{1,0:T(8,128)S(1)}, u32[]{:S(2)}, u32[]{:S(2)}) collective-permute-start(f32[7,2048]{1,0:T(8,128)S(1)} %add.85), channel_id=1, source_target_pairs={{0,4},{1,5},{2,6},{3,7},{4,0},{5,1},{6,2},{7,3},{8,12},{9,13},{10,... | collective-permute-start | bytes 172040 | tf_op jit(solution)/shard_map/ppermute | solution.py:26
  198.9 23.3 %collective-permute-start.6 = (f32[512,3,16]{0,2,1:T(8,128)S(1)}, f32[512,3,16]{0,2,1:T(8,128)S(1)}, u32[]{:S(2)}, u32[]{:S(2)}) collective-permute-start(f32[512,3,16]{0,2,1:T(8,128)S(1)} %maximum_select_fusion.2), channel_id=1, source_target_pairs={{0,4},{1,5},{2,6},{3,7},{4,0},{5,1},{6,2},{7,3},{8,12},{9,13},{10,... | collective-permute-start | bytes 294920 | tf_op jit(solution)/shard_map/ppermute | solution.py:37
  200.5 20.4 %collective-permute-start.11 = (f32[7,2048]{1,0:T(8,128)S(1)}, f32[7,2048]{1,0:T(8,128)S(1)}, u32[]{:S(2)}, u32[]{:S(2)}) collective-permute-start(f32[7,2048]{1,0:T(8,128)S(1)} %add.86), channel_id=1, source_target_pairs={{0,8},{1,9},{2,10},{3,11},{4,12},{5,13},{6,14},{7,15},{8,0},{9,1},... | collective-permute-start | bytes 172040 | tf_op jit(solution)/shard_map/ppermute | solution.py:26
  220.9 3.6 %collective-permute-start.12 = (f32[7,2048]{1,0:T(8,128)S(1)}, f32[7,2048]{1,0:T(8,128)S(1)}, u32[]{:S(2)}, u32[]{:S(2)}) collective-permute-start(f32[7,2048]{1,0:T(8,128)S(1)} %add.87), channel_id=1, source_target_pairs={{0,16},{1,17},{2,18},{3,19},{4,20},{5,21},{6,22},{7,23},{8,24},{9,... | collective-permute-start | bytes 172040 | tf_op jit(solution)/shard_map/ppermute | solution.py:26
  222.3 13.3 %collective-permute-start.7 = (f32[1024,3,16]{0,2,1:T(8,128)S(1)}, f32[1024,3,16]{0,2,1:T(8,128)S(1)}, u32[]{:S(2)}, u32[]{:S(2)}) collective-permute-start(f32[1024,3,16]{0,2,1:T(8,128)S(1)} %maximum_select_fusion.1), channel_id=1, source_target_pairs={{0,8},{1,9},{2,10},{3,11},{4,12},{5,13},{6,14},{7,15},{8,0},{9,1},... | collective-permute-start | bytes 589832 | tf_op jit(solution)/shard_map/ppermute | solution.py:37
  224.5 7.4 %collective-permute-start.13 = (f32[7,2048]{1,0:T(8,128)S(1)}, f32[7,2048]{1,0:T(8,128)S(1)}, u32[]{:S(2)}, u32[]{:S(2)}) collective-permute-start(f32[7,2048]{1,0:T(8,128)S(1)} %add.88), channel_id=1, source_target_pairs={{0,32},{1,33},{2,34},{3,35},{4,36},{5,37},{6,38},{7,39},{8,40},{9,... | collective-permute-start | bytes 172040 | tf_op jit(solution)/shard_map/ppermute | solution.py:26
  231.9 7.1 %collective-permute-start.14 = (f32[7,2048]{1,0:T(8,128)S(1)}, f32[7,2048]{1,0:T(8,128)S(1)}, u32[]{:S(2)}, u32[]{:S(2)}) collective-permute-start(f32[7,2048]{1,0:T(8,128)S(1)} %add.89), channel_id=1, source_target_pairs={{0,64},{1,65},{2,66},{3,67},{4,68},{5,69},{6,70},{7,71},{8,72},{9,... | collective-permute-start | bytes 172040 | tf_op jit(solution)/shard_map/ppermute | solution.py:26
  239.0 17.6 %collective-permute-start.15 = (f32[7,2048]{1,0:T(8,128)S(1)}, f32[7,2048]{1,0:T(8,128)S(1)}, u32[]{:S(2)}, u32[]{:S(2)}) collective-permute-start(f32[7,2048]{1,0:T(8,128)S(1)} %add.90), channel_id=1, source_target_pairs={{0,128},{1,129},{2,130},{3,131},{4,132},{5,133},{6,134},{7,135},{8... | collective-permute-start | bytes 172040 | tf_op jit(solution)/shard_map/ppermute | solution.py:26
  241.7 23.5 %copy-start = (bf16[128,16,128]{2,0,1:T(8,128)(2,1)S(1)}, bf16[128,16,128]{2,0,1:T(8,128)(2,1)}, u32[]{:S(2)}) copy-start(bf16[128,16,128]{2,0,1:T(8,128)(2,1)} %copy.81) | copy-start | bytes 1572868
Sparse Core Ops, SparseCore 0:
  10.4 58.8 all-gather.4
  71.7 66.7 all-gather.6
  140.3 63.5 all-gather.8
  205.5 59.5 all-gather.10
where the time goes:
time: 304 us; the launch traced here: 299 us
  waiting for transfers between devices  135 us (44%)
  matrix products  93 us (31%)
  other arithmetic  22.2 us (7%)
  starting transfers between devices  18.6 us (6%)
  local copies, waits for them, and re-layouts  15.5 us (5%)
  between operations  14.5 us (5%)
    all_gather x1, waiting for transfers between devices, on_device(): k_heads = lax.all_gather(head_major(local_k), 'seq', axis=1, tiled=True)  58.6 us
    ppermute x2, waiting for transfers between devices, padded(): before = lax.ppermute(value[length - width:], 'seq', up)  22.6 us
    ppermute x2, waiting for transfers between devices, padded(): after = lax.ppermute(value[:width], 'seq', down)  22.6 us
    dot_general x1, matrix products, on_device(): jnp.einsum('htu,hud->thd', dscore, k_heads, preferred_element_type=jnp.fl...  17.1 us
    dot_general x1, matrix products, on_device(): jnp.einsum('thd,hud->htu', d_heads, v_heads, preferred_element_type=jnp.f...  16 us
    dot_general x1, matrix products, on_device(): jnp.einsum('hud,htd->hut', kq_heads, qa_heads, preferred_element_type=jnp...  15 us
    dot_general x1, matrix products, on_device(): jnp.einsum('hut,htd->uhd', dscore_t, qa_heads, preferred_element_type=jnp...  13.5 us
    ppermute x8, starting transfers between devices, butterfly_sum(): value = value + lax.ppermute(value, axes, pairs)  13.2 us
  transfers between devices with their start and end apart: 20, of which 12 were waited for; matrix products, arithmetic and copies ran while one was open for 34% of the time, Pallas kernels for 0%

commit v1 on v0

--- a/solution.py
+++ b/solution.py
@@ -73,8 +73,8 @@
     k_heads, local_v = lax.optimization_barrier((k_heads, local_v))
     v_heads = lax.all_gather(head_major(local_v), "seq", axis=1, tiled=True)
 
-    q_heads = local_q.reshape(tok_rows, head_count, HD)
-    d_heads = grad_attn.reshape(tok_rows, head_count, HD)
+    q_heads = head_major(local_q)
+    d_heads = head_major(grad_attn)
 
     device_index = lax.axis_index("seq")
     own_pos = device_index * tok_rows + jnp.arange(tok_rows, dtype=jnp.int32)
@@ -82,7 +82,7 @@
     visible = own_pos[:, None] >= all_pos[None, :]
 
     scores = (
-        jnp.einsum("thd,hud->htu", q_heads, k_heads, preferred_element_type=jnp.float32)
+        jnp.einsum("htd,hud->htu", q_heads, k_heads, preferred_element_type=jnp.float32)
         * score_scale
     )
     row_top = jnp.max(jnp.where(visible, scores, -jnp.inf), -1, keepdims=True)
@@ -96,7 +96,7 @@
     da_heads = lax.all_gather(head_major(grad_attn2), "seq", axis=1, tiled=True)
     attended = jnp.einsum("htu,hud->thd", probs_low, v_heads, preferred_element_type=jnp.float32)
     attn_out = attended.astype(jnp.bfloat16).reshape(tok_rows, channels)
-    dprob = jnp.einsum("thd,hud->htu", d_heads, v_heads, preferred_element_type=jnp.float32)
+    dprob = jnp.einsum("htd,hud->htu", d_heads, v_heads, preferred_element_type=jnp.float32)
     row_delta = jnp.sum(probs * dprob, -1, keepdims=True)
     dscore = (probs * (dprob - row_delta) * score_scale).astype(jnp.bfloat16)
     grad_q = jnp.einsum("htu,hud->thd", dscore, k_heads, preferred_element_type=jnp.float32)

time: 304 us -> 304 us (level)
  no operation moved by 1% of the time
where the time goes in v1:
time: 304 us; the launch traced here: 299 us
  waiting for transfers between devices  135 us (44%)
  matrix products  93 us (31%)
  other arithmetic  22.1 us (7%)
  starting transfers between devices  18.6 us (6%)
  local copies, waits for them, and re-layouts  15.8 us (5%)
  between operations  14.5 us (5%)
    all_gather x1, waiting for transfers between devices, on_device(): k_heads = lax.all_gather(head_major(local_k), 'seq', axis=1, tiled=True)  58.6 us
    ppermute x2, waiting for transfers between devices, padded(): before = lax.ppermute(value[length - width:], 'seq', up)  22.6 us
    ppermute x2, waiting for transfers between devices, padded(): after = lax.ppermute(value[:width], 'seq', down)  22.6 us
    dot_general x1, matrix products, on_device(): jnp.einsum('htu,hud->thd', dscore, k_heads, preferred_element_type=jnp.fl...  17.1 us
    dot_general x1, matrix products, on_device(): jnp.einsum('htd,hud->htu', d_heads, v_heads, preferred_element_type=jnp.f...  16 us
    dot_general x1, matrix products, on_device(): jnp.einsum('hud,htd->hut', kq_heads, qa_heads, preferred_element_type=jnp...  15 us
    dot_general x1, matrix products, on_device(): jnp.einsum('hut,htd->uhd', dscore_t, qa_heads, preferred_element_type=jnp...  13.5 us
    ppermute x8, starting transfers between devices, butterfly_sum(): value = value + lax.ppermute(value, axes, pairs)  13.2 us
  transfers between devices with their start and end apart: 20, of which 12 were waited for; matrix products, arithmetic and copies ran while one was open for 34% of the time, Pallas kernels for 0%

profile of v1, /device:TPU:1, one launch (start us, length us, event | category | flops | bytes accessed | tf_op | source)
XLA Modules:
  0.0 298.6 jit_solution(17135562503651405740)
XLA Ops:
  7.2 1.1 copy.118
  8.4 0.9 copy.128
  9.4 1.3 copy.80
  10.7 58.6 %all-gather.5.cloned.1.call-done = bf16[16,2048,128]{2,1,0:T(8,128)(2,1)} async-done(((bf16[16,128,128]{2,1,0:T(8,128)(2,1)}), bf16[16,2048,128]{2,1,0:T(8,128)(2,1)}) %all-gather.5.cloned.1.call-update) | async-done | bytes 8388624 | tf_op jit(solution)/shard_map/all_gather | solution.py:72
  69.3 1.0 copy.81
  70.4 1.3 copy.83
  71.7 1.1 copy.119
  72.9 1.0 iota_compare_fusion
  73.9 11.8 %fusion.1 = (f32[16,128]{1,0:T(8,128)S(1)}, f32[16,2048,128]{2,1,0:T(8,128)}) fusion(pred[128,2048]{0,1:T(8,128)(4,1)S(1)} %get-tuple-element.63, bf16[16,2048,128]{2,1,0:T(8,128)(2,1)} %all-gather.5.cloned.1.call-done, bf16[128,16,128]{2,1,0:T(8,128)(2,1)S(1)} %bitcast.149), kind=kOutput, calls=%fused_computation.4 | convolution fusion | flops 1086322688 | bytes 25960448 | tf_op jit(solution)/shard_map/htd,hud->htu/dot_general | solution.py:85
  85.7 1.0 copy.96
  87.3 1.4 collective-permute-start.1
  88.9 22.6 %collective-permute-done.1 = bf16[3,2048]{0,1:T(8,128)(2,1)S(1)} collective-permute-done((bf16[3,2048]{0,1:T(8,128)(2,1)S(1)}, bf16[3,2048]{0,1:T(8,128)(2,1)S(1)}, u32[]{:S(2)}, u32[]{:S(2)}) %collective-permute-start.1) | collective-permute-done | bytes 12320 | tf_op jit(solution)/shard_map/ppermute | solution.py:15
  111.5 3.1 %collective-permute-done = bf16[3,2048]{0,1:T(8,128)(2,1)S(1)} collective-permute-done((bf16[3,2048]{0,1:T(8,128)(2,1)S(1)}, bf16[3,2048]{0,1:T(8,128)(2,1)S(1)}, u32[]{:S(2)}, u32[]{:S(2)}) %collective-permute-start) | collective-permute-done | bytes 12320 | tf_op jit(solution)/shard_map/ppermute | solution.py:16
  114.7 3.7 %fusion.33 = bf16[128,2048]{0,1:T(8,128)(2,1)S(1)} fusion(bf16[128,2048]{0,1:T(8,128)(2,1)S(1)} %bitcast.131, bf16[3,2048]{0,1:T(8,128)(2,1)S(1)} %collective-permute-done.1, bf16[3,2048]{0,1:T(8,128)(2,1)S(1)} %collective-permute-done, f32[2048]{0:T(1024)S(1)} %bitcast.161, f32[2048]{0:T(1024)S(1)} %bitcast.163, f32[2048]{0:T(1024)S(1)} %bitcast.153, ...), kind=kLoop, calls=%fused_computation.66 | loop fusion | flops 10223616 | bytes 1130496 | tf_op jit(solution)/shard_map/convert_element_type | solution.py:67
  118.7 9.5 %fusion.5 = f32[16,128]{1,0:T(8,128)S(1)} fusion(f32[16,2048,128]{2,1,0:T(8,128)} %get-tuple-element.65, f32[16,128]{1,0:T(8,128)S(1)} %get-tuple-element.64, pred[128,2048]{0,1:T(8,128)(4,1)S(1)} %get-tuple-element.63), kind=kLoop, calls=%fused_computation.11 | loop fusion | flops 16775168 | bytes 17055744 | tf_op jit(solution)/shard_map/reduce_sum | solution.py:92
  128.2 10.3 %all-gather.7.cloned.1.call-done = bf16[16,2048,128]{2,1,0:T(8,128)(2,1)} async-done(((bf16[16,128,128]{2,1,0:T(8,128)(2,1)}), bf16[16,2048,128]{2,1,0:T(8,128)(2,1)}) %all-gather.7.cloned.1.call-update) | async-done | bytes 8388624 | tf_op jit(solution)/shard_map/all_gather | solution.py:74
  138.5 16.0 %multiply_reduce_fusion = (f32[16,128]{1,0:T(8,128)S(1)}, bf16[16,128,2048]{1,2,0:T(8,128)(2,1)}, f32[16,128,2048]{1,2,0:T(8,128)}) fusion(f32[16,128]{1,0:T(8,128)S(1)} %fusion.5, f32[16,128]{1,0:T(8,128)S(1)} %get-tuple-element.64, f32[16,2048,128]{2,1,0:T(8,128)} %get-tuple-element.65, pred[128,2048]{0,1:T(8,128)(4,1)S(1)} %get-tuple-element.63, ...), kind=kOutput, calls=%fused_computation.9 | convolution fusion | flops 1103099904 | bytes 51142656 | tf_op jit(solution)/shard_map/htd,hud->htu/dot_general | solution.py:99
  154.5 1.0 copy.97
  155.8 8.8 %multiply_reduce_fusion.1 = (f32[16,128]{1,0:T(8,128)S(1)}, bf16[128,16,128]{2,0,1:T(8,128)(2,1)S(1)}) fusion(f32[128,16,128]{2,0,1:T(8,128)S(1)} %copy.104, bf16[16,2048,128]{2,1,0:T(8,128)(2,1)} %all-gather.7.cloned.1.call-done, bf16[16,128,2048]{1,2,0:T(8,128)(2,1)} %get-tuple-element.14), kind=kOutput, calls=%fused_computation.73 | convolution fusion | flops 1074788352 | bytes 18358272 | tf_op jit(solution)/shard_map/htu,hud->thd/dot_general | solution.py:97
  164.6 1.1 copy.90
  165.7 0.7 collective-permute-start.3
  167.0 19.5 %collective-permute-done.3 = bf16[3,2048]{0,1:T(8,128)(2,1)S(1)} collective-permute-done((bf16[3,2048]{0,1:T(8,128)(2,1)}, bf16[3,2048]{0,1:T(8,128)(2,1)S(1)}, u32[]{:S(2)}, u32[]{:S(2)}) %collective-permute-start.3) | collective-permute-done | bytes 12320 | tf_op jit(solution)/shard_map/ppermute | solution.py:16
  186.5 3.4 %fusion.39 = (f32[2048]{0:T(1024)S(1)}, f32[2048]{0:T(1024)S(1)}, f32[2048]{0:T(1024)S(1)}, f32[2048]{0:T(1024)S(1)}, f32[2048]{0:T(1024)S(1)}, /*index=5*/f32[2048]{0:T(1024)S(1)}) fusion(bf16[3,2048]{0,1:T(8,128)(2,1)S(1)} %collective-permute-done.3, bf16[128,2048]{0,1:T(8,128)(2,1)S(1)} %bitcast.136, bf16[1,128,2048]{1,2,0:T(8,128)(2,1)S(1)} %copy.84, ...), kind=kLoop, calls=%fused_computation.72 | loop fusion | flops 9687040 | bytes 1122304 | tf_op jit(solution)/shard_map/reduce_sum | solution.py:135
  190.1 0.5 collective-permute-start.4
  190.6 0.7 collective-permute-done.8
  191.7 1.3 collective-permute-start.5
  193.0 3.8 %collective-permute-done.9 = f32[7,2048]{1,0:T(8,128)S(1)} collective-permute-done((f32[7,2048]{1,0:T(8,128)S(1)}, f32[7,2048]{1,0:T(8,128)S(1)}, u32[]{:S(2)}, u32[]{:S(2)}) %collective-permute-start.9) | collective-permute-done | bytes 57376 | tf_op jit(solution)/shard_map/ppermute | solution.py:26
  196.9 2.0 collective-permute-done.5
  199.0 1.4 collective-permute-done.10
  200.5 2.4 collective-permute-start.11
  202.8 17.1 %fusion.20 = bf16[16,128,128]{2,1,0:T(8,128)(2,1)S(1)} fusion(bf16[16,2048,128]{2,1,0:T(8,128)(2,1)} %all-gather.5.cloned.1.call-done, f32[16,128,2048]{1,2,0:T(8,128)} %get-tuple-element.66, f32[16,128]{1,0:T(8,128)S(1)} %get-tuple-element.46, f32[16,2048,128]{2,1,0:T(8,128)} %get-tuple-element.65, f32[16,128]{1,0:T(8,128)S(1)} %fusion.5, ...), kind=kOutput, calls=%fused_computation.37 | convolution fusion | flops 1107558400 | bytes 42754048 | tf_op jit(solution)/shard_map/htu,hud->thd/dot_general | solution.py:102
  219.9 1.0 copy.106
  220.9 1.4 collective-permute-start.12
  222.3 1.0 collective-permute-start.7
  223.3 1.3 collective-permute-done.12
  224.6 2.6 collective-permute-start.13
  227.2 3.7 %fusion.53 = bf16[1,128,2048]{1,2,0:T(8,128)(2,1)S(1)} fusion(f32[2048]{0:T(1024)S(1)} %bitcast.162, f32[2048]{0:T(1024)S(1)} %bitcast.164, f32[2048]{0:T(1024)S(1)} %bitcast.154, bf16[128,2048]{0,1:T(8,128)(2,1)S(1)} %bitcast.137, f32[2048]{0:T(1024)S(1)} %bitcast.156, f32[2048]{0:T(1024)S(1)} %bitcast.158, f32[2048]{0:T(1024)S(1)} %bitcast.160, ...), kind=kLoop, calls=%fused_computation.96 | loop fusion | flops 10223616 | bytes 1130496 | tf_op jit(solution)/shard_map/broadcast_in_dim | solution.py:139
  230.9 1.0 copy.105
  231.9 3.8 %collective-permute-start.14 = (f32[7,2048]{1,0:T(8,128)S(1)}, f32[7,2048]{1,0:T(8,128)S(1)}, u32[]{:S(2)}, u32[]{:S(2)}) collective-permute-start(f32[7,2048]{1,0:T(8,128)S(1)} %add.89), channel_id=1, source_target_pairs={{0,64},{1,65},{2,66},{3,67},{4,68},{5,69},{6,70},{7,71},{8,72},{9,... | collective-permute-start | bytes 172040 | tf_op jit(solution)/shard_map/ppermute | solution.py:26
  235.8 3.3 %collective-permute-done.14 = f32[7,2048]{1,0:T(8,128)S(1)} collective-permute-done((f32[7,2048]{1,0:T(8,128)S(1)}, f32[7,2048]{1,0:T(8,128)S(1)}, u32[]{:S(2)}, u32[]{:S(2)}) %collective-permute-start.14) | collective-permute-done | bytes 57376 | tf_op jit(solution)/shard_map/ppermute | solution.py:26
  239.0 2.6 collective-permute-start.15
  241.7 15.0 %fusion = f32[16,128,2048]{1,2,0:T(8,128)} fusion(f32[16,2048]{1,0:T(8,128)S(1)} %get-tuple-element.53, f32[16,2048]{1,0:T(8,128)S(1)} %get-tuple-element.54, pred[128,2048]{0,1:T(8,128)(4,1)} %get-tuple-element.62, bf16[16,2048,128]{2,1,0:T(8,128)(2,1)} %all-gather.9.cloned.1.call-done, bf16[128,16,128]{2,1,0:T(8,128)(2,1)S(1)} %bitcast.142), kind=kOutput, calls=%fused_computation.1 | convolution fusion | flops 1090519040 | bytes 26214400 | tf_op jit(solution)/shard_map/hud,htd->hut/dot_general | solution.py:115
  256.6 0.6 add.91
  257.3 7.9 %all-gather.11.cloned.1.call-done = bf16[16,2048,128]{2,1,0:T(8,128)(2,1)} async-done(((bf16[16,128,128]{2,1,0:T(8,128)(2,1)}), bf16[16,2048,128]{2,1,0:T(8,128)(2,1)}) %all-gather.11.cloned.1.call-update) | async-done | bytes 8388624 | tf_op jit(solution)/shard_map/all_gather | solution.py:96
  265.2 13.5 %fusion.19 = bf16[16,128,128]{2,1,0:T(8,128)(2,1)S(1)} fusion(bf16[16,2048,128]{2,1,0:T(8,128)(2,1)} %all-gather.9.cloned.1.call-done, f32[16,128,2048]{1,2,0:T(8,128)} %fusion, f32[16,2048]{1,0:T(8,128)S(1)} %get-tuple-element.52, bf16[16,2048,128]{2,1,0:T(8,128)(2,1)} %all-gather.11.cloned.1.call-done, bf16[128,16,128]{2,0,1:T(8,128)(2,1)S(1)} %copy-done), kind=kOutput, calls=%fused_computation.35 | convolution fusion | flops 2164523008 | bytes 34734080 | tf_op jit(solution)/shard_map/hut,htd->uhd/dot_general | solution.py:123
  278.7 1.0 copy.107
  279.7 10.9 %fusion.16 = bf16[16,128,128]{2,1,0:T(8,128)(2,1)S(1)} fusion(bf16[16,2048,128]{2,1,0:T(8,128)(2,1)} %all-gather.11.cloned.1.call-done, f32[16,128,2048]{1,2,0:T(8,128)} %fusion), kind=kOutput, calls=%fused_computation.34 | convolution fusion | flops 1078198272 | bytes 25690112 | tf_op jit(solution)/shard_map/hut,htd->uhd/dot_general | solution.py:124
  290.7 1.0 copy.108
  (51 shorter events, 3.0 us)
Async XLA Ops:
  7.2 62.1 %all-gather.5.cloned.1.call-start = ((), (), s32[]{:S(2)}) async-start(), calls=%async_computation | async-start | bytes 8912896 | tf_op jit(solution)/shard_map/all_gather | solution.py:72
  9.3 129.2 %all-gather.7.cloned.1.call-start = ((), (), s32[]{:S(2)}) async-start(), calls=%async_computation.1 | async-start | bytes 8912896 | tf_op jit(solution)/shard_map/all_gather | solution.py:74
  70.3 171.3 %all-gather.9.cloned.1.call-start = ((), (), s32[]{:S(2)}) async-start(), calls=%async_computation.2 | async-start | bytes 8912896 | tf_op jit(solution)/shard_map/all_gather | solution.py:90
  73.9 12.9 %copy-start.1 = (bf16[1,128,2048]{2,1,0:T(8,128)(2,1)S(1)}, bf16[1,128,2048]{2,1,0:T(8,128)(2,1)}, u32[]{:S(2)}) copy-start(bf16[1,128,2048]{2,1,0:T(8,128)(2,1)} %param.8) | copy-start | bytes 1572868
  73.9 15.0 %copy-start.2 = (f32[7,2048]{1,0:T(8,128)S(1)}, f32[7,2048]{1,0:T(8,128)}, u32[]{:S(2)}) copy-start(f32[7,2048]{1,0:T(8,128)} %param.9) | copy-start | bytes 172036
  86.7 178.4 %all-gather.11.cloned.1.call-start = ((), (), s32[]{:S(2)}) async-start(), calls=%async_computation.3 | async-start | bytes 8912896 | tf_op jit(solution)/shard_map/all_gather | solution.py:96
  87.3 24.3 %collective-permute-start.1 = (bf16[3,2048]{0,1:T(8,128)(2,1)S(1)}, bf16[3,2048]{0,1:T(8,128)(2,1)S(1)}, u32[]{:S(2)}, u32[]{:S(2)}) collective-permute-start(bf16[3,2048]{0,1:T(8,128)(2,1)S(1)} %get-tuple-element.51), channel_id=1, source_target_pairs={{0,1},{1,2},{2,3},{3,4},{4,5},{5,6},{6,7},{7,8},{8,9},{9,10},{10,1... | collective-permute-start | bytes 36872 | tf_op jit(solution)/shard_map/ppermute | solution.py:15
  88.7 26.0 %collective-permute-start = (bf16[3,2048]{0,1:T(8,128)(2,1)S(1)}, bf16[3,2048]{0,1:T(8,128)(2,1)S(1)}, u32[]{:S(2)}, u32[]{:S(2)}) collective-permute-start(bf16[3,2048]{0,1:T(8,128)(2,1)S(1)} %get-tuple-element.50), channel_id=1, source_target_pairs={{1,0},{2,1},{3,2},{4,3},{5,4},{6,5},{7,6},{8,7},{9,8},{10,9},{11,1... | collective-permute-start | bytes 36872 | tf_op jit(solution)/shard_map/ppermute | solution.py:16
  164.5 2.1 collective-permute-start.2
  165.7 20.8 %collective-permute-start.3 = (bf16[3,2048]{0,1:T(8,128)(2,1)}, bf16[3,2048]{0,1:T(8,128)(2,1)S(1)}, u32[]{:S(2)}, u32[]{:S(2)}) collective-permute-start(bf16[3,2048]{0,1:T(8,128)(2,1)} %copy.90), channel_id=1, source_target_pairs={{1,0},{2,1},{3,2},{4,3},{5,4},{6,5},{7,6},{8,7},{9,8},{10,9},{11,1... | collective-permute-start | bytes 36872 | tf_op jit(solution)/shard_map/ppermute | solution.py:16
  190.0 1.3 collective-permute-start.8
  190.1 1.6 collective-permute-start.4
  191.3 5.5 %collective-permute-start.9 = (f32[7,2048]{1,0:T(8,128)S(1)}, f32[7,2048]{1,0:T(8,128)S(1)}, u32[]{:S(2)}, u32[]{:S(2)}) collective-permute-start(f32[7,2048]{1,0:T(8,128)S(1)} %add.84), channel_id=1, source_target_pairs={{0,2},{1,3},{2,0},{3,1},{4,6},{5,7},{6,4},{7,5},{8,10},{9,11},{10,... | collective-permute-start | bytes 172040 | tf_op jit(solution)/shard_map/ppermute | solution.py:26
  191.7 7.3 %collective-permute-start.5 = (f32[256,3,16]{0,2,1:T(8,128)S(1)}, f32[256,3,16]{0,2,1:T(8,128)S(1)}, u32[]{:S(2)}, u32[]{:S(2)}) collective-permute-start(f32[256,3,16]{0,2,1:T(8,128)S(1)} %maximum_select_fusion.3), channel_id=1, source_target_pairs={{0,2},{1,3},{2,0},{3,1},{4,6},{5,7},{6,4},{7,5},{8,10},{9,11},{10,... | collective-permute-start | bytes 147464 | tf_op jit(solution)/shard_map/ppermute | solution.py:37
  196.8 3.6 %collective-permute-start.10 = (f32[7,2048]{1,0:T(8,128)S(1)}, f32[7,2048]{1,0:T(8,128)S(1)}, u32[]{:S(2)}, u32[]{:S(2)}) collective-permute-start(f32[7,2048]{1,0:T(8,128)S(1)} %add.85), channel_id=1, source_target_pairs={{0,4},{1,5},{2,6},{3,7},{4,0},{5,1},{6,2},{7,3},{8,12},{9,13},{10,... | collective-permute-start | bytes 172040 | tf_op jit(solution)/shard_map/ppermute | solution.py:26
  198.9 23.3 %collective-permute-start.6 = (f32[512,3,16]{0,2,1:T(8,128)S(1)}, f32[512,3,16]{0,2,1:T(8,128)S(1)}, u32[]{:S(2)}, u32[]{:S(2)}) collective-permute-start(f32[512,3,16]{0,2,1:T(8,128)S(1)} %maximum_select_fusion.2), channel_id=1, source_target_pairs={{0,4},{1,5},{2,6},{3,7},{4,0},{5,1},{6,2},{7,3},{8,12},{9,13},{10,... | collective-permute-start | bytes 294920 | tf_op jit(solution)/shard_map/ppermute | solution.py:37
  200.5 20.5 %collective-permute-start.11 = (f32[7,2048]{1,0:T(8,128)S(1)}, f32[7,2048]{1,0:T(8,128)S(1)}, u32[]{:S(2)}, u32[]{:S(2)}) collective-permute-start(f32[7,2048]{1,0:T(8,128)S(1)} %add.86), channel_id=1, source_target_pairs={{0,8},{1,9},{2,10},{3,11},{4,12},{5,13},{6,14},{7,15},{8,0},{9,1},... | collective-permute-start | bytes 172040 | tf_op jit(solution)/shard_map/ppermute | solution.py:26
  220.9 3.6 %collective-permute-start.12 = (f32[7,2048]{1,0:T(8,128)S(1)}, f32[7,2048]{1,0:T(8,128)S(1)}, u32[]{:S(2)}, u32[]{:S(2)}) collective-permute-start(f32[7,2048]{1,0:T(8,128)S(1)} %add.87), channel_id=1, source_target_pairs={{0,16},{1,17},{2,18},{3,19},{4,20},{5,21},{6,22},{7,23},{8,24},{9,... | collective-permute-start | bytes 172040 | tf_op jit(solution)/shard_map/ppermute | solution.py:26
  222.3 13.4 %collective-permute-start.7 = (f32[1024,3,16]{0,2,1:T(8,128)S(1)}, f32[1024,3,16]{0,2,1:T(8,128)S(1)}, u32[]{:S(2)}, u32[]{:S(2)}) collective-permute-start(f32[1024,3,16]{0,2,1:T(8,128)S(1)} %maximum_select_fusion.1), channel_id=1, source_target_pairs={{0,8},{1,9},{2,10},{3,11},{4,12},{5,13},{6,14},{7,15},{8,0},{9,1},... | collective-permute-start | bytes 589832 | tf_op jit(solution)/shard_map/ppermute | solution.py:37
  224.6 7.4 %collective-permute-start.13 = (f32[7,2048]{1,0:T(8,128)S(1)}, f32[7,2048]{1,0:T(8,128)S(1)}, u32[]{:S(2)}, u32[]{:S(2)}) collective-permute-start(f32[7,2048]{1,0:T(8,128)S(1)} %add.88), channel_id=1, source_target_pairs={{0,32},{1,33},{2,34},{3,35},{4,36},{5,37},{6,38},{7,39},{8,40},{9,... | collective-permute-start | bytes 172040 | tf_op jit(solution)/shard_map/ppermute | solution.py:26
  231.9 7.1 %collective-permute-start.14 = (f32[7,2048]{1,0:T(8,128)S(1)}, f32[7,2048]{1,0:T(8,128)S(1)}, u32[]{:S(2)}, u32[]{:S(2)}) collective-permute-start(f32[7,2048]{1,0:T(8,128)S(1)} %add.89), channel_id=1, source_target_pairs={{0,64},{1,65},{2,66},{3,67},{4,68},{5,69},{6,70},{7,71},{8,72},{9,... | collective-permute-start | bytes 172040 | tf_op jit(solution)/shard_map/ppermute | solution.py:26
  239.0 17.6 %collective-permute-start.15 = (f32[7,2048]{1,0:T(8,128)S(1)}, f32[7,2048]{1,0:T(8,128)S(1)}, u32[]{:S(2)}, u32[]{:S(2)}) collective-permute-start(f32[7,2048]{1,0:T(8,128)S(1)} %add.90), channel_id=1, source_target_pairs={{0,128},{1,129},{2,130},{3,131},{4,132},{5,133},{6,134},{7,135},{8... | collective-permute-start | bytes 172040 | tf_op jit(solution)/shard_map/ppermute | solution.py:26
  241.7 23.5 %copy-start = (bf16[128,16,128]{2,0,1:T(8,128)(2,1)S(1)}, bf16[128,16,128]{2,0,1:T(8,128)(2,1)}, u32[]{:S(2)}) copy-start(bf16[128,16,128]{2,0,1:T(8,128)(2,1)} %copy.81) | copy-start | bytes 1572868
Sparse Core Ops, SparseCore 0:
  10.4 58.8 all-gather.4
  71.7 66.7 all-gather.6
  140.3 63.5 all-gather.8
  205.5 59.5 all-gather.10
